TPU v7x, 512 devices: a whole 4x8x8 slice. The times are simulated.
512 devices in a mesh: row: 16 (over y, x_lo), col: 16 (over z, core), ka: 2 (over x_hi).
Axes of the slice: x: 4 (x_hi: 2, x_lo: 2; x = x_hi * 2 + x_lo), y: 8, z: 8, core: 2. Of those that a mesh axis runs over, the one named last changes fastest.
Arguments:
- pair: bfloat16 [512, 512, 128], P('row', ('col', 'ka')), may hold values from -6 to 6
- pair_mask: int32 [512, 512], P('row', ('col', 'ka')), may hold values from 0 to 1, as said below
- w_in: bfloat16 [2, 128, 512], replicated, may hold values from -0.5 to 0.5
- w_gate: bfloat16 [2, 128, 128], replicated, may hold values from -0.5 to 0.5
- w_out: bfloat16 [2, 128, 128], replicated, may hold values from -0.5 to 0.5
Outputs:
- updated: bfloat16 [512, 512, 128], P('row', ('col', 'ka'))
Inputs may be any that keep to these rules, and one draw needn't show every extreme that they name: pair_mask[i, j] = v[i] v[j] for a per-token 0/1 validity v; within each aligned run of 16 tokens the real tokens come first and there is at least one.
All inputs are finite; a program needn't handle non-finite values.
Results may differ from a plain program's by a relative error of at most 0.014.
Values may be sent and summed in bfloat16 or wider, within the bound.
No kernel may reach another device: no remote copies, remote signals or barrier semaphores. Data moves between devices by JAX's collectives and lax.ppermute only.
A program may use at most 64 MiB of HBM per device.

v0:
```python
import jax
import jax.numpy as jnp
from jax import lax
from jax.sharding import PartitionSpec as P


def layer_norm(value):
    mean = jnp.mean(value, axis=-1, keepdims=True)
    centred = value - mean
    var = jnp.mean(centred * centred, axis=-1, keepdims=True)
    return centred / jnp.sqrt(var + 1e-05)


def prepare(pair, valid, weight_in, weight_gate):
    normed = layer_norm(pair.astype(jnp.float32)).astype(jnp.bfloat16)
    proj = jnp.einsum("ijc,cd->ijd", normed, weight_in, preferred_element_type=jnp.float32)
    width = proj.shape[-1] // 4
    left = (jax.nn.sigmoid(proj[..., :width]) * proj[..., width : 2 * width] * valid).astype(
        jnp.bfloat16
    )
    right = (
        jax.nn.sigmoid(proj[..., 2 * width : 3 * width]) * proj[..., 3 * width :] * valid
    ).astype(jnp.bfloat16)
    gate = jax.nn.sigmoid(
        jnp.einsum("ijc,cd->ijd", normed, weight_gate, preferred_element_type=jnp.float32)
    )
    return (left, right, gate)


def finish(pair, tri, gate, weight_out):
    normed = layer_norm(tri).astype(jnp.bfloat16)
    proj = jnp.einsum("ijc,cd->ijd", normed, weight_out, preferred_element_type=jnp.float32)
    return (pair.astype(jnp.float32) + gate * proj).astype(jnp.bfloat16)


def transpose_tiles(value, n):
    perm = [(r * n + c, c * n + r) for r in range(n) for c in range(n)]
    return lax.ppermute(value, ("row", "col"), perm)


def on_device(n, pair, pair_mask, w_in, w_gate, w_out):
    valid = pair_mask.astype(jnp.float32)[..., None]
    left, right, gate = prepare(pair, valid, w_in[0], w_gate[0])
    left_rows = lax.all_gather(left, "col", axis=1, tiled=True)
    right_diag = lax.all_gather(transpose_tiles(right, n), "row", axis=1, tiled=True)
    partial_value = jnp.einsum(
        "ikc,jkc->ijc", left_rows, right_diag, preferred_element_type=jnp.float32
    )
    tri = lax.psum_scatter(
        partial_value.astype(jnp.bfloat16), "ka", scatter_dimension=1, tiled=True
    ).astype(jnp.float32)
    middle = finish(pair, tri, gate, w_out[0])
    left, right, gate = prepare(middle, valid, w_in[1], w_gate[1])
    right_cols = lax.all_gather(right, "row", axis=0, tiled=True)
    left_half = lax.all_gather(transpose_tiles(left, n), "col", axis=0, tiled=True)
    left_diag = lax.all_gather(left_half, "ka", axis=1, tiled=True)
    tri = jnp.einsum("kic,kjc->ijc", left_diag, right_cols, preferred_element_type=jnp.float32)
    return finish(middle, tri, gate, w_out[1])


def solution(mesh):
    n = mesh.shape["row"]
    assert mesh.shape["col"] == n
    placed = (P("row", ("col", "ka"), None), P("row", ("col", "ka")), P(), P(), P())
    return jax.shard_map(
        lambda *a: on_device(n, *a),
        mesh=mesh,
        in_specs=placed,
        out_specs=P("row", ("col", "ka"), None),
        check_vma=False,
    )
```

profile of v0, /device:TPU:1, one launch (start us, length us, event | category | flops | bytes accessed | tf_op | source)
XLA Modules:
  0.0 423.1 jit_solution(14155994391619889289)
XLA Ops:
  6.5 1.0 convert_reduce_fusion.1
  7.7 1.1 fusion.18
  9.8 1.3 fusion.42
  12.1 4.5 %collective-permute-start = (bf16[32,16,128]{2,1,0:T(8,128)(2,1)S(1)}, bf16[32,16,128]{2,1,0:T(8,128)(2,1)S(1)}, u32[]{:S(2)}, u32[]{:S(2)}) collective-permute-start(bf16[32,16,128]{2,1,0:T(8,128)(2,1)S(1)} %get-tuple-element.8), channel_id=1, source_target_pairs={{0,0},{2,32},{4,64},{6,96},{8,128},{10,160},{12,192},{14,224},{16,... | collective-permute-start | bytes 393224 | tf_op jit(solution)/shard_map/ppermute | solution.py:38
  16.6 2.6 collective-permute-done
  19.9 45.1 %all-gather.8.cloned.1.call-done = bf16[32,256,128]{2,1,0:T(8,128)(2,1)} async-done(((bf16[32,16,128]{2,1,0:T(8,128)(2,1)}), bf16[32,256,128]{2,1,0:T(8,128)(2,1)}) %all-gather.8.cloned.1.call-update) | async-done | bytes 2097168 | tf_op jit(solution)/shard_map/all_gather | solution.py:44
  65.1 15.2 %copy.49 = bf16[32,256,128]{0,1,2:T(8,128)(2,1)} copy(bf16[32,256,128]{2,1,0:T(8,128)(2,1)} %all-gather.8.cloned.1.call-done) | data formatting | bytes 4194304 | tf_op jit(solution)/shard_map/all_gather | solution.py:44
  80.3 57.6 %all-gather.6.cloned.1.call-done = bf16[32,256,128]{2,1,0:T(8,128)(2,1)} async-done(((bf16[32,16,128]{2,1,0:T(8,128)(2,1)}), bf16[32,256,128]{2,1,0:T(8,128)(2,1)}) %all-gather.6.cloned.1.call-update) | async-done | bytes 2097168 | tf_op jit(solution)/shard_map/all_gather | solution.py:45
  137.9 15.2 %copy.48 = bf16[32,256,128]{0,1,2:T(8,128)(2,1)} copy(bf16[32,256,128]{2,1,0:T(8,128)(2,1)} %all-gather.6.cloned.1.call-done) | data formatting | bytes 4194304 | tf_op jit(solution)/shard_map/all_gather | solution.py:45
  153.2 9.2 %fusion = bf16[32,32,128]{0,1,2:T(8,128)(2,1)} fusion(bf16[32,256,128]{0,1,2:T(8,128)(2,1)} %copy.48, bf16[32,256,128]{0,1,2:T(8,128)(2,1)} %copy.49), kind=kOutput, calls=%fused_computation.1 | convolution fusion | flops 67239936 | bytes 4456448 | tf_op jit(solution)/shard_map/ikc,jkc->ijc/dot_general | solution.py:46
  162.8 39.5 %reduce-scatter.2.cloned.1.call-done = bf16[32,16,128]{0,1,2:T(8,128)(2,1)} async-done(((bf16[32,32,128]{0,1,2:T(8,128)(2,1)}), bf16[32,16,128]{0,1,2:T(8,128)(2,1)}) %reduce-scatter.2.cloned.1.call-update) | async-done | bytes 131088 | tf_op jit(solution)/shard_map/reduce_scatter | solution.py:49
  202.3 1.2 convert_reduce_fusion
  203.5 1.3 fusion.14
  204.8 1.2 fusion.15
  207.7 0.8 fusion.21
  208.5 2.9 collective-permute-start.1
  211.4 3.4 collective-permute-done.1
  216.1 53.4 %all-gather.12.cloned.1.call-done = bf16[512,16,128]{2,1,0:T(8,128)(2,1)} async-done(((bf16[32,16,128]{2,1,0:T(8,128)(2,1)}), bf16[512,16,128]{2,1,0:T(8,128)(2,1)}) %all-gather.12.cloned.1.call-update) | async-done | bytes 2097168 | tf_op jit(solution)/shard_map/all_gather | solution.py:55
  269.5 4.9 %copy.55 = bf16[512,16,128]{0,1,2:T(8,128)(2,1)} copy(bf16[512,16,128]{2,1,0:T(8,128)(2,1)} %all-gather.12.cloned.1.call-done) | data formatting | bytes 4194304 | tf_op jit(solution)/shard_map/all_gather | solution.py:55
  274.8 59.3 %all-gather.10.cloned.1.call-done = bf16[512,16,128]{2,1,0:T(8,128)(2,1)} async-done(((bf16[32,16,128]{2,1,0:T(8,128)(2,1)}), bf16[512,16,128]{2,1,0:T(8,128)(2,1)}) %all-gather.10.cloned.1.call-update) | async-done | bytes 2097168 | tf_op jit(solution)/shard_map/all_gather | solution.py:54
  334.1 3.9 copy.56
  338.0 73.1 %all-gather.14.cloned.1.call-done = bf16[512,32,128]{0,1,2:T(8,128)(2,1)} async-done(((bf16[512,16,128]{0,1,2:T(8,128)(2,1)}), bf16[512,32,128]{0,1,2:T(8,128)(2,1)}) %all-gather.14.cloned.1.call-update) | async-done | bytes 4194320 | tf_op jit(solution)/shard_map/all_gather | solution.py:56
  411.1 3.4 fusion.57
  415.4 0.8 fusion.13
  (52 shorter events, 7.3 us)
Async XLA Ops:
  6.5 58.5 %all-gather.8.cloned.1.call-start = ((), (), s32[]{:S(2)}) async-start(), calls=%async_computation.2 | async-start | bytes 2228224 | tf_op jit(solution)/shard_map/all_gather | solution.py:44
  12.0 125.9 %all-gather.6.cloned.1.call-start = ((), (), s32[]{:S(2)}) async-start(), calls=%async_computation.1 | async-start | bytes 2228224 | tf_op jit(solution)/shard_map/all_gather | solution.py:45
  12.1 7.1 %collective-permute-start = (bf16[32,16,128]{2,1,0:T(8,128)(2,1)S(1)}, bf16[32,16,128]{2,1,0:T(8,128)(2,1)S(1)}, u32[]{:S(2)}, u32[]{:S(2)}) collective-permute-start(bf16[32,16,128]{2,1,0:T(8,128)(2,1)S(1)} %get-tuple-element.8), channel_id=1, source_target_pairs={{0,0},{2,32},{4,64},{6,96},{8,128},{10,160},{12,192},{14,224},{16,... | collective-permute-start | bytes 393224 | tf_op jit(solution)/shard_map/ppermute | solution.py:38
  19.2 0.7 copy-start.3
  19.9 182.4 %reduce-scatter.2.cloned.1.call-start = ((), (), s32[]{:S(2)}) async-start(), calls=%async_computation.3 | async-start | bytes 1572864 | tf_op jit(solution)/shard_map/reduce_scatter | solution.py:49
  153.2 9.3 %copy-start = (bf16[32,16,128]{2,1,0:T(8,128)(2,1)S(1)}, bf16[32,16,128]{2,1,0:T(8,128)(2,1)}, u32[]{:S(2)}) copy-start(bf16[32,16,128]{2,1,0:T(8,128)(2,1)} %param.5) | copy-start | bytes 393220
  153.2 9.3 %copy-start.5 = (bf16[2,128,128]{2,1,0:T(8,128)(2,1)S(1)}, bf16[2,128,128]{2,1,0:T(8,128)(2,1)}, u32[]{:S(2)}) copy-start(bf16[2,128,128]{2,1,0:T(8,128)(2,1)} %param.8) | copy-start | bytes 196612
  162.3 44.1 %copy-start.4 = (bf16[2,128,128]{2,1,0:T(8,128)(2,1)S(1)}, bf16[2,128,128]{2,1,0:T(8,128)(2,1)}, u32[]{:S(2)}) copy-start(bf16[2,128,128]{2,1,0:T(8,128)(2,1)} %param.9) | copy-start | bytes 196612
  162.3 45.0 %copy-start.1 = (bf16[2,128,512]{2,1,0:T(8,128)(2,1)S(1)}, bf16[2,128,512]{2,1,0:T(8,128)(2,1)}, u32[]{:S(2)}) copy-start(bf16[2,128,512]{2,1,0:T(8,128)(2,1)} %param.7) | copy-start | bytes 786436
  162.4 107.2 %all-gather.12.cloned.1.call-start = ((), (), s32[]{:S(2)}) async-start(), calls=%async_computation.5 | async-start | bytes 2228224 | tf_op jit(solution)/shard_map/all_gather | solution.py:55
  208.5 6.3 %collective-permute-start.1 = (bf16[32,16,128]{2,1,0:T(8,128)(2,1)S(1)}, bf16[32,16,128]{2,1,0:T(8,128)(2,1)S(1)}, u32[]{:S(2)}, u32[]{:S(2)}) collective-permute-start(bf16[32,16,128]{2,1,0:T(8,128)(2,1)S(1)} %get-tuple-element.5), channel_id=1, source_target_pairs={{0,0},{2,32},{4,64},{6,96},{8,128},{10,160},{12,192},{14,224},{16,... | collective-permute-start | bytes 393224 | tf_op jit(solution)/shard_map/ppermute | solution.py:38
  214.8 0.6 copy-start.2
  215.5 118.6 %all-gather.10.cloned.1.call-start = ((), (), s32[]{:S(2)}) async-start(), calls=%async_computation.4 | async-start | bytes 2228224 | tf_op jit(solution)/shard_map/all_gather | solution.py:54
  216.1 195.1 %all-gather.14.cloned.1.call-start = ((), (), s32[]{:S(2)}) async-start(), calls=%async_computation.6 | async-start | bytes 6291456 | tf_op jit(solution)/shard_map/all_gather | solution.py:56
Sparse Core Ops, SparseCore 0:
  12.1 52.8 all-gather.7
  67.1 70.8 all-gather.5
  162.5 39.7 reduce-scatter.1
  215.6 53.8 all-gather.11
  271.5 62.6 all-gather.9
  336.1 75.0 all-gather.13
where the time goes:
time: 424 us; the launch traced here: 423 us
  waiting for transfers between devices  335 us (79%)
  local copies, waits for them, and re-layouts  42.3 us (10%)
  matrix products  16 us (4%)
  between operations  13.6 us (3%)
  other arithmetic  8.84 us (2%)
  starting transfers between devices  7.61 us (2%)
    all_gather x1, waiting for transfers between devices, on_device(): left_diag = lax.all_gather(left_half, 'ka', axis=1, tiled=True)  73.1 us
    all_gather x1, waiting for transfers between devices, on_device(): right_cols = lax.all_gather(right, 'row', axis=0, tiled=True)  59.3 us
    all_gather x1, waiting for transfers between devices, on_device(): lax.all_gather(transpose_tiles(right, n), 'row', axis=1, tiled=True)  57.6 us
    all_gather x1, waiting for transfers between devices, on_device(): lax.all_gather(transpose_tiles(left, n), 'col', axis=0, tiled=True)  53.4 us
    all_gather x1, waiting for transfers between devices, on_device(): left_rows = lax.all_gather(left, 'col', axis=1, tiled=True)  45.1 us
    reduce_scatter x1, waiting for transfers between devices, on_device(): lax.psum_scatter(partial_value.astype(jnp.bfloat16), 'ka', scatter_dimens...  39.5 us
    all_gather x1, local copies, waits for them, and re-layouts, on_device(): left_rows = lax.all_gather(left, 'col', axis=1, tiled=True)  15.2 us
    all_gather x1, local copies, waits for them, and re-layouts, on_device(): lax.all_gather(transpose_tiles(right, n), 'row', axis=1, tiled=True)  15.2 us
  transfers between devices with their start and end apart: 8, of which 8 were waited for; matrix products, arithmetic and copies ran while one was open for 6% of the time, Pallas kernels for 0%

commit v1 on v0

--- a/solution.py
+++ b/solution.py
@@ -2,6 +2,22 @@
 import jax.numpy as jnp
 from jax import lax
 from jax.sharding import PartitionSpec as P
+
+
+def ring_product(x, axis, dim, term):
+    size, position, span = (lax.axis_size(axis), lax.axis_index(axis), x.shape[dim])
+    right = [(i, (i + 1) % size) for i in range(size)]
+    left = [(i, (i - 1) % size) for i in range(size)]
+    half = size // 2
+    from_left = from_right = x
+    so_far = term(x, position * span)
+    for step in range(1, half + 1):
+        from_left = lax.ppermute(from_left, axis, right)
+        if step < size - half:
+            from_right = lax.ppermute(from_right, axis, left)
+            so_far = so_far + term(from_right, (position + step) % size * span)
+        so_far = so_far + term(from_left, (position - step) % size * span)
+    return so_far
 
 
 def layer_norm(value):
@@ -41,10 +57,17 @@
 def on_device(n, pair, pair_mask, w_in, w_gate, w_out):
     valid = pair_mask.astype(jnp.float32)[..., None]
     left, right, gate = prepare(pair, valid, w_in[0], w_gate[0])
-    left_rows = lax.all_gather(left, "col", axis=1, tiled=True)
     right_diag = lax.all_gather(transpose_tiles(right, n), "row", axis=1, tiled=True)
-    partial_value = jnp.einsum(
-        "ikc,jkc->ijc", left_rows, right_diag, preferred_element_type=jnp.float32
+    partial_value = ring_product(
+        left,
+        "col",
+        1,
+        lambda part, start: jnp.einsum(
+            "ikc,jkc->ijc",
+            part,
+            lax.dynamic_slice_in_dim(right_diag, start, part.shape[1], axis=1),
+            preferred_element_type=jnp.float32,
+        ),
     )
     tri = lax.psum_scatter(
         partial_value.astype(jnp.bfloat16), "ka", scatter_dimension=1, tiled=True

time: 424 us -> 437 us (1.031)
  waiting for transfers between devices: 335 us -> 260 us
  starting transfers between devices: 7.61 us -> 50.7 us
  local copies, waits for them, and re-layouts: 42.3 us -> 69.9 us
  matrix products: 16 us -> 33.5 us
    all_gather x1 -> x0, waiting for transfers between devices: 45.1 us -> none  [on_device(): left_rows = lax.all_gather(left, 'col', axis=1, tiled=True)]
    ppermute x0 -> x15, starting transfers between devices: none -> 42.9 us  [the longest x7 35.2 us: ring_product(): from_right = lax.ppermute(from_right, axis, left)]
    all_gather x1, waiting for transfers between devices: 57.6 us -> 18.9 us  [on_device(): lax.all_gather(transpose_tiles(right, n), 'row', axis=1, tiled=True)]
    dynamic_slice x0 -> x17, local copies, waits for them, and re-layouts: none -> 36.4 us  [on_device(): lax.dynamic_slice_in_dim(right_diag, start, part.shape[1], axis=1)]
    all_gather x2 -> x0, local copies, waits for them, and re-layouts: 30.5 us -> none  [the longest x1 15.2 us: on_device(): left_rows = lax.all_gather(left, 'col', axis=1, tiled=True)]
    dot_general x1 -> x16, matrix products: 9.18 us -> 25.7 us  [on_device(): jnp.einsum('ikc,jkc->ijc', part, lax.dynamic_slice_in_dim(right_diag, sta...]
    ppermute x0 -> x15, local copies, waits for them, and re-layouts: none -> 15 us  [the longest x8 7.8 us: ring_product(): from_left = lax.ppermute(from_left, axis, right)]
    ppermute x0 -> x15, waiting for transfers between devices: none -> 11.3 us  [the longest x8 8.29 us: ring_product(): from_left = lax.ppermute(from_left, axis, right)]
  transfers between devices with their start and end apart: 8 -> 22, of which waited for: 8 -> 20; matrix products, arithmetic and copies ran while one was open for 6% -> 6% of each run, Pallas kernels for 0% -> 0%
where the time goes in v1:
time: 437 us; the launch traced here: 436 us
  waiting for transfers between devices  260 us (59%)
  local copies, waits for them, and re-layouts  69.9 us (16%)
  starting transfers between devices  50.7 us (12%)
  matrix products  33.5 us (8%)
  between operations  13.5 us (3%)
  other arithmetic  8.19 us (2%)
    all_gather x1, waiting for transfers between devices, on_device(): left_diag = lax.all_gather(left_half, 'ka', axis=1, tiled=True)  73.1 us
    all_gather x1, waiting for transfers between devices, on_device(): right_cols = lax.all_gather(right, 'row', axis=0, tiled=True)  58.5 us
    all_gather x1, waiting for transfers between devices, on_device(): lax.all_gather(transpose_tiles(left, n), 'col', axis=0, tiled=True)  53.4 us
    reduce_scatter x1, waiting for transfers between devices, on_device(): lax.psum_scatter(partial_value.astype(jnp.bfloat16), 'ka', scatter_dimens...  38.3 us
    dynamic_slice x17, local copies, waits for them, and re-layouts, on_device(): lax.dynamic_slice_in_dim(right_diag, start, part.shape[1], axis=1)  36.4 us
    ppermute x7, starting transfers between devices, ring_product(): from_right = lax.ppermute(from_right, axis, left)  35.2 us
    dot_general x16, matrix products, on_device(): jnp.einsum('ikc,jkc->ijc', part, lax.dynamic_slice_in_dim(right_diag, sta...  25.7 us
    all_gather x1, waiting for transfers between devices, on_device(): lax.all_gather(transpose_tiles(right, n), 'row', axis=1, tiled=True)  18.9 us
  transfers between devices with their start and end apart: 22, of which 20 were waited for; matrix products, arithmetic and copies ran while one was open for 6% of the time, Pallas kernels for 0%

profile of v1, /device:TPU:1, one launch (start us, length us, event | category | flops | bytes accessed | tf_op | source)
XLA Modules:
  0.0 435.9 jit_solution(8963251332249827258)
XLA Ops:
  11.4 4.5 %collective-permute-start = (bf16[32,16,128]{2,1,0:T(8,128)(2,1)S(1)}, bf16[32,16,128]{2,1,0:T(8,128)(2,1)S(1)}, u32[]{:S(2)}, u32[]{:S(2)}) collective-permute-start(bf16[32,16,128]{2,1,0:T(8,128)(2,1)S(1)} %get-tuple-element.24), channel_id=1, source_target_pairs={{0,0},{2,32},{4,64},{6,96},{8,128},{10,160},{12,192},{14,224},{16,... | collective-permute-start | bytes 393224 | tf_op jit(solution)/shard_map/ppermute | solution.py:54
  15.9 2.6 collective-permute-done
  19.2 5.1 %collective-permute-start.2 = (bf16[32,16,128]{2,1,0:T(8,128)(2,1)S(1)}, bf16[32,16,128]{2,1,0:T(8,128)(2,1)S(1)}, u32[]{:S(2)}, u32[]{:S(2)}) collective-permute-start(bf16[32,16,128]{2,1,0:T(8,128)(2,1)S(1)} %get-tuple-element.23), channel_id=1, source_target_pairs={{0,2},{2,4},{4,6},{6,8},{8,10},{10,12},{12,14},{14,16},{16,18},{18... | collective-permute-start | bytes 393224 | tf_op jit(solution)/shard_map/ppermute | solution.py:15
  24.4 4.2 collective-permute-done.2
  28.5 2.5 collective-permute-start.4
  32.7 11.8 %collective-permute-start.3 = (bf16[32,16,128]{2,1,0:T(8,128)(2,1)S(1)}, bf16[32,16,128]{2,1,0:T(8,128)(2,1)S(1)}, u32[]{:S(2)}, u32[]{:S(2)}) collective-permute-start(bf16[32,16,128]{2,1,0:T(8,128)(2,1)S(1)} %collective-permute-done.1), channel_id=1, source_target_pairs={{0,30},{2,0},{4,2},{6,4},{8,6},{10,8},{12,10},{14,12},{16,14},{18,... | collective-permute-start | bytes 393224 | tf_op jit(solution)/shard_map/ppermute | solution.py:17
  45.5 4.6 %collective-permute-start.5 = (bf16[32,16,128]{2,1,0:T(8,128)(2,1)S(1)}, bf16[32,16,128]{2,1,0:T(8,128)(2,1)S(1)}, u32[]{:S(2)}, u32[]{:S(2)}) collective-permute-start(bf16[32,16,128]{2,1,0:T(8,128)(2,1)S(1)} %collective-permute-done.3), channel_id=1, source_target_pairs={{0,30},{2,0},{4,2},{6,4},{8,6},{10,8},{12,10},{14,12},{16,14},{18,... | collective-permute-start | bytes 393224 | tf_op jit(solution)/shard_map/ppermute | solution.py:17
  51.1 4.6 %collective-permute-start.7 = (bf16[32,16,128]{2,1,0:T(8,128)(2,1)S(1)}, bf16[32,16,128]{2,1,0:T(8,128)(2,1)S(1)}, u32[]{:S(2)}, u32[]{:S(2)}) collective-permute-start(bf16[32,16,128]{2,1,0:T(8,128)(2,1)S(1)} %collective-permute-done.5), channel_id=1, source_target_pairs={{0,30},{2,0},{4,2},{6,4},{8,6},{10,8},{12,10},{14,12},{16,14},{18,... | collective-permute-start | bytes 393224 | tf_op jit(solution)/shard_map/ppermute | solution.py:17
  56.7 4.9 %collective-permute-start.9 = (bf16[32,16,128]{2,1,0:T(8,128)(2,1)S(1)}, bf16[32,16,128]{2,1,0:T(8,128)(2,1)S(1)}, u32[]{:S(2)}, u32[]{:S(2)}) collective-permute-start(bf16[32,16,128]{2,1,0:T(8,128)(2,1)S(1)} %collective-permute-done.7), channel_id=1, source_target_pairs={{0,30},{2,0},{4,2},{6,4},{8,6},{10,8},{12,10},{14,12},{16,14},{18,... | collective-permute-start | bytes 393224 | tf_op jit(solution)/shard_map/ppermute | solution.py:17
  62.6 4.6 %collective-permute-start.11 = (bf16[32,16,128]{2,1,0:T(8,128)(2,1)S(1)}, bf16[32,16,128]{2,1,0:T(8,128)(2,1)S(1)}, u32[]{:S(2)}, u32[]{:S(2)}) collective-permute-start(bf16[32,16,128]{2,1,0:T(8,128)(2,1)S(1)} %collective-permute-done.9), channel_id=1, source_target_pairs={{0,30},{2,0},{4,2},{6,4},{8,6},{10,8},{12,10},{14,12},{16,14},{18,... | collective-permute-start | bytes 393224 | tf_op jit(solution)/shard_map/ppermute | solution.py:17
  68.2 4.6 %collective-permute-start.13 = (bf16[32,16,128]{2,1,0:T(8,128)(2,1)S(1)}, bf16[32,16,128]{2,1,0:T(8,128)(2,1)S(1)}, u32[]{:S(2)}, u32[]{:S(2)}) collective-permute-start(bf16[32,16,128]{2,1,0:T(8,128)(2,1)S(1)} %collective-permute-done.11), channel_id=1, source_target_pairs={{0,30},{2,0},{4,2},{6,4},{8,6},{10,8},{12,10},{14,12},{16,14},{18,... | collective-permute-start | bytes 393224 | tf_op jit(solution)/shard_map/ppermute | solution.py:17
  89.6 18.9 %all-gather.5.cloned.1.call-done = bf16[32,256,128]{2,1,0:T(8,128)(2,1)} async-done(((bf16[32,16,128]{2,1,0:T(8,128)(2,1)}), bf16[32,256,128]{2,1,0:T(8,128)(2,1)}) %all-gather.5.cloned.1.call-update) | async-done | bytes 2097168 | tf_op jit(solution)/shard_map/all_gather | solution.py:60
  108.6 2.9 constant_dynamic-slice_fusion.14
  129.1 2.4 copy.148
  167.0 8.4 %fusion = bf16[32,32,128]{0,1,2:T(8,128)(2,1)} fusion(bf16[32,16,128]{0,1,2:T(8,128)(2,1)} %copy.168, bf16[32,16,128]{0,1,2:T(8,128)(2,1)S(1)} %copy.169, f32[128,32,32]{2,1,0:T(8,128)S(1)} %fusion.72, f32[128,32,32]{2,1,0:T(8,128)S(1)} %fusion.71, f32[128,32,32]{2,1,0:T(8,128)S(1)} %fusion.70, f32[128,32,32]{2,1,0:T(8,128)S(1)} %fusion.69, ...), kind=kOutput, calls=%fused_computation.1 | convolution fusion | flops 6291456 | bytes 8388608 | tf_op jit(solution)/shard_map/ikc,jkc->ijc/dot_general | solution.py:65
  177.1 38.3 %reduce-scatter.2.cloned.1.call-done = bf16[32,16,128]{0,1,2:T(8,128)(2,1)} async-done(((bf16[32,32,128]{0,1,2:T(8,128)(2,1)}), bf16[32,16,128]{0,1,2:T(8,128)(2,1)}) %reduce-scatter.2.cloned.1.call-update) | async-done | bytes 131088 | tf_op jit(solution)/shard_map/reduce_scatter | solution.py:72
  221.6 2.9 collective-permute-start.16
  224.5 3.4 collective-permute-done.16
  229.2 53.4 %all-gather.9.cloned.1.call-done = bf16[512,16,128]{2,1,0:T(8,128)(2,1)} async-done(((bf16[32,16,128]{2,1,0:T(8,128)(2,1)}), bf16[512,16,128]{2,1,0:T(8,128)(2,1)}) %all-gather.9.cloned.1.call-update) | async-done | bytes 2097168 | tf_op jit(solution)/shard_map/all_gather | solution.py:78
  282.6 4.9 %copy.175 = bf16[512,16,128]{0,1,2:T(8,128)(2,1)} copy(bf16[512,16,128]{2,1,0:T(8,128)(2,1)} %all-gather.9.cloned.1.call-done) | data formatting | bytes 4194304 | tf_op jit(solution)/shard_map/all_gather | solution.py:78
  288.8 58.5 %all-gather.7.cloned.1.call-done = bf16[512,16,128]{2,1,0:T(8,128)(2,1)} async-done(((bf16[32,16,128]{2,1,0:T(8,128)(2,1)}), bf16[512,16,128]{2,1,0:T(8,128)(2,1)}) %all-gather.7.cloned.1.call-update) | async-done | bytes 2097168 | tf_op jit(solution)/shard_map/all_gather | solution.py:77
  347.2 3.9 copy.176
  351.2 73.1 %all-gather.11.cloned.1.call-done = bf16[512,32,128]{0,1,2:T(8,128)(2,1)} async-done(((bf16[512,16,128]{0,1,2:T(8,128)(2,1)}), bf16[512,32,128]{0,1,2:T(8,128)(2,1)}) %all-gather.11.cloned.1.call-update) | async-done | bytes 4194320 | tf_op jit(solution)/shard_map/all_gather | solution.py:79
  424.2 3.4 fusion.57
  (177 shorter events, 93.7 us)
Async XLA Ops:
  6.5 102.0 %all-gather.5.cloned.1.call-start = ((), (), s32[]{:S(2)}) async-start(), calls=%async_computation.1 | async-start | bytes 2228224 | tf_op jit(solution)/shard_map/all_gather | solution.py:60
  9.9 66.0 %copy-start.25 = (f32[32,16]{1,0:T(8,128)}, f32[32,16]{1,0:T(8,128)S(1)}, u32[]{:S(2)}) copy-start(f32[32,16]{1,0:T(8,128)S(1)} %copy.137) | copy-start | bytes 6148
  11.4 7.1 %collective-permute-start = (bf16[32,16,128]{2,1,0:T(8,128)(2,1)S(1)}, bf16[32,16,128]{2,1,0:T(8,128)(2,1)S(1)}, u32[]{:S(2)}, u32[]{:S(2)}) collective-permute-start(bf16[32,16,128]{2,1,0:T(8,128)(2,1)S(1)} %get-tuple-element.24), channel_id=1, source_target_pairs={{0,0},{2,32},{4,64},{6,96},{8,128},{10,160},{12,192},{14,224},{16,... | collective-permute-start | bytes 393224 | tf_op jit(solution)/shard_map/ppermute | solution.py:54
  19.2 196.2 %reduce-scatter.2.cloned.1.call-start = ((), (), s32[]{:S(2)}) async-start(), calls=%async_computation.2 | async-start | bytes 1572864 | tf_op jit(solution)/shard_map/reduce_scatter | solution.py:72
  19.2 9.3 %collective-permute-start.2 = (bf16[32,16,128]{2,1,0:T(8,128)(2,1)S(1)}, bf16[32,16,128]{2,1,0:T(8,128)(2,1)S(1)}, u32[]{:S(2)}, u32[]{:S(2)}) collective-permute-start(bf16[32,16,128]{2,1,0:T(8,128)(2,1)S(1)} %get-tuple-element.23), channel_id=1, source_target_pairs={{0,2},{2,4},{4,6},{6,8},{8,10},{10,12},{12,14},{14,16},{16,18},{18... | collective-permute-start | bytes 393224 | tf_op jit(solution)/shard_map/ppermute | solution.py:15
  24.4 8.3 %collective-permute-start.1 = (bf16[32,16,128]{2,1,0:T(8,128)(2,1)S(1)}, bf16[32,16,128]{2,1,0:T(8,128)(2,1)S(1)}, u32[]{:S(2)}, u32[]{:S(2)}) collective-permute-start(bf16[32,16,128]{2,1,0:T(8,128)(2,1)S(1)} %get-tuple-element.23), channel_id=1, source_target_pairs={{0,30},{2,0},{4,2},{6,4},{8,6},{10,8},{12,10},{14,12},{16,14},{18,... | collective-permute-start | bytes 393224 | tf_op jit(solution)/shard_map/ppermute | solution.py:17
  28.5 16.8 %collective-permute-start.4 = (bf16[32,16,128]{2,1,0:T(8,128)(2,1)S(1)}, bf16[32,16,128]{2,1,0:T(8,128)(2,1)S(1)}, u32[]{:S(2)}, u32[]{:S(2)}) collective-permute-start(bf16[32,16,128]{2,1,0:T(8,128)(2,1)S(1)} %collective-permute-done.2), channel_id=1, source_target_pairs={{0,2},{2,4},{4,6},{6,8},{8,10},{10,12},{12,14},{14,16},{16,18},{18... | collective-permute-start | bytes 393224 | tf_op jit(solution)/shard_map/ppermute | solution.py:15
  32.7 12.8 %collective-permute-start.3 = (bf16[32,16,128]{2,1,0:T(8,128)(2,1)S(1)}, bf16[32,16,128]{2,1,0:T(8,128)(2,1)S(1)}, u32[]{:S(2)}, u32[]{:S(2)}) collective-permute-start(bf16[32,16,128]{2,1,0:T(8,128)(2,1)S(1)} %collective-permute-done.1), channel_id=1, source_target_pairs={{0,30},{2,0},{4,2},{6,4},{8,6},{10,8},{12,10},{14,12},{16,14},{18,... | collective-permute-start | bytes 393224 | tf_op jit(solution)/shard_map/ppermute | solution.py:17
  45.4 5.6 %collective-permute-start.6 = (bf16[32,16,128]{2,1,0:T(8,128)(2,1)S(1)}, bf16[32,16,128]{2,1,0:T(8,128)(2,1)S(1)}, u32[]{:S(2)}, u32[]{:S(2)}) collective-permute-start(bf16[32,16,128]{2,1,0:T(8,128)(2,1)S(1)} %collective-permute-done.4), channel_id=1, source_target_pairs={{0,2},{2,4},{4,6},{6,8},{8,10},{10,12},{12,14},{14,16},{16,18},{18... | collective-permute-start | bytes 393224 | tf_op jit(solution)/shard_map/ppermute | solution.py:15
  45.5 5.6 %collective-permute-start.5 = (bf16[32,16,128]{2,1,0:T(8,128)(2,1)S(1)}, bf16[32,16,128]{2,1,0:T(8,128)(2,1)S(1)}, u32[]{:S(2)}, u32[]{:S(2)}) collective-permute-start(bf16[32,16,128]{2,1,0:T(8,128)(2,1)S(1)} %collective-permute-done.3), channel_id=1, source_target_pairs={{0,30},{2,0},{4,2},{6,4},{8,6},{10,8},{12,10},{14,12},{16,14},{18,... | collective-permute-start | bytes 393224 | tf_op jit(solution)/shard_map/ppermute | solution.py:17
  51.0 5.6 %collective-permute-start.8 = (bf16[32,16,128]{2,1,0:T(8,128)(2,1)S(1)}, bf16[32,16,128]{2,1,0:T(8,128)(2,1)S(1)}, u32[]{:S(2)}, u32[]{:S(2)}) collective-permute-start(bf16[32,16,128]{2,1,0:T(8,128)(2,1)S(1)} %collective-permute-done.6), channel_id=1, source_target_pairs={{0,2},{2,4},{4,6},{6,8},{8,10},{10,12},{12,14},{14,16},{16,18},{18... | collective-permute-start | bytes 393224 | tf_op jit(solution)/shard_map/ppermute | solution.py:15
  51.1 5.6 %collective-permute-start.7 = (bf16[32,16,128]{2,1,0:T(8,128)(2,1)S(1)}, bf16[32,16,128]{2,1,0:T(8,128)(2,1)S(1)}, u32[]{:S(2)}, u32[]{:S(2)}) collective-permute-start(bf16[32,16,128]{2,1,0:T(8,128)(2,1)S(1)} %collective-permute-done.5), channel_id=1, source_target_pairs={{0,30},{2,0},{4,2},{6,4},{8,6},{10,8},{12,10},{14,12},{16,14},{18,... | collective-permute-start | bytes 393224 | tf_op jit(solution)/shard_map/ppermute | solution.py:17
  56.6 5.6 %collective-permute-start.10 = (bf16[32,16,128]{2,1,0:T(8,128)(2,1)S(1)}, bf16[32,16,128]{2,1,0:T(8,128)(2,1)S(1)}, u32[]{:S(2)}, u32[]{:S(2)}) collective-permute-start(bf16[32,16,128]{2,1,0:T(8,128)(2,1)S(1)} %collective-permute-done.8), channel_id=1, source_target_pairs={{0,2},{2,4},{4,6},{6,8},{8,10},{10,12},{12,14},{14,16},{16,18},{18... | collective-permute-start | bytes 393224 | tf_op jit(solution)/shard_map/ppermute | solution.py:15
  56.7 5.9 %collective-permute-start.9 = (bf16[32,16,128]{2,1,0:T(8,128)(2,1)S(1)}, bf16[32,16,128]{2,1,0:T(8,128)(2,1)S(1)}, u32[]{:S(2)}, u32[]{:S(2)}) collective-permute-start(bf16[32,16,128]{2,1,0:T(8,128)(2,1)S(1)} %collective-permute-done.7), channel_id=1, source_target_pairs={{0,30},{2,0},{4,2},{6,4},{8,6},{10,8},{12,10},{14,12},{16,14},{18,... | collective-permute-start | bytes 393224 | tf_op jit(solution)/shard_map/ppermute | solution.py:17
  62.2 5.6 %collective-permute-start.12 = (bf16[32,16,128]{2,1,0:T(8,128)(2,1)S(1)}, bf16[32,16,128]{2,1,0:T(8,128)(2,1)S(1)}, u32[]{:S(2)}, u32[]{:S(2)}) collective-permute-start(bf16[32,16,128]{2,1,0:T(8,128)(2,1)S(1)} %collective-permute-done.10), channel_id=1, source_target_pairs={{0,2},{2,4},{4,6},{6,8},{8,10},{10,12},{12,14},{14,16},{16,18},{18... | collective-permute-start | bytes 393224 | tf_op jit(solution)/shard_map/ppermute | solution.py:15
  62.6 5.6 %collective-permute-start.11 = (bf16[32,16,128]{2,1,0:T(8,128)(2,1)S(1)}, bf16[32,16,128]{2,1,0:T(8,128)(2,1)S(1)}, u32[]{:S(2)}, u32[]{:S(2)}) collective-permute-start(bf16[32,16,128]{2,1,0:T(8,128)(2,1)S(1)} %collective-permute-done.9), channel_id=1, source_target_pairs={{0,30},{2,0},{4,2},{6,4},{8,6},{10,8},{12,10},{14,12},{16,14},{18,... | collective-permute-start | bytes 393224 | tf_op jit(solution)/shard_map/ppermute | solution.py:17
  67.8 5.6 %collective-permute-start.14 = (bf16[32,16,128]{2,1,0:T(8,128)(2,1)S(1)}, bf16[32,16,128]{2,1,0:T(8,128)(2,1)S(1)}, u32[]{:S(2)}, u32[]{:S(2)}) collective-permute-start(bf16[32,16,128]{2,1,0:T(8,128)(2,1)S(1)} %collective-permute-done.12), channel_id=1, source_target_pairs={{0,2},{2,4},{4,6},{6,8},{8,10},{10,12},{12,14},{14,16},{16,18},{18... | collective-permute-start | bytes 393224 | tf_op jit(solution)/shard_map/ppermute | solution.py:15
  68.2 18.7 %collective-permute-start.13 = (bf16[32,16,128]{2,1,0:T(8,128)(2,1)S(1)}, bf16[32,16,128]{2,1,0:T(8,128)(2,1)S(1)}, u32[]{:S(2)}, u32[]{:S(2)}) collective-permute-start(bf16[32,16,128]{2,1,0:T(8,128)(2,1)S(1)} %collective-permute-done.11), channel_id=1, source_target_pairs={{0,30},{2,0},{4,2},{6,4},{8,6},{10,8},{12,10},{14,12},{16,14},{18,... | collective-permute-start | bytes 393224 | tf_op jit(solution)/shard_map/ppermute | solution.py:17
  73.4 14.8 %collective-permute-start.15 = (bf16[32,16,128]{2,1,0:T(8,128)(2,1)S(1)}, bf16[32,16,128]{2,1,0:T(8,128)(2,1)}, u32[]{:S(2)}, u32[]{:S(2)}) collective-permute-start(bf16[32,16,128]{2,1,0:T(8,128)(2,1)S(1)} %collective-permute-done.14), channel_id=1, source_target_pairs={{0,2},{2,4},{4,6},{6,8},{8,10},{10,12},{12,14},{14,16},{16,18},{18... | collective-permute-start | bytes 393224 | tf_op jit(solution)/shard_map/ppermute | solution.py:15
  175.5 44.0 %copy-start.23 = (bf16[32,16,128]{2,1,0:T(8,128)(2,1)S(1)}, bf16[32,16,128]{2,1,0:T(8,128)(2,1)}, u32[]{:S(2)}) copy-start(bf16[32,16,128]{2,1,0:T(8,128)(2,1)} %param.5) | copy-start | bytes 393220
  175.5 107.1 %all-gather.9.cloned.1.call-start = ((), (), s32[]{:S(2)}) async-start(), calls=%async_computation.4 | async-start | bytes 2228224 | tf_op jit(solution)/shard_map/all_gather | solution.py:78
  221.6 6.3 %collective-permute-start.16 = (bf16[32,16,128]{2,1,0:T(8,128)(2,1)S(1)}, bf16[32,16,128]{2,1,0:T(8,128)(2,1)S(1)}, u32[]{:S(2)}, u32[]{:S(2)}) collective-permute-start(bf16[32,16,128]{2,1,0:T(8,128)(2,1)S(1)} %get-tuple-element.21), channel_id=1, source_target_pairs={{0,0},{2,32},{4,64},{6,96},{8,128},{10,160},{12,192},{14,224},{16,... | collective-permute-start | bytes 393224 | tf_op jit(solution)/shard_map/ppermute | solution.py:54
  228.6 118.7 %all-gather.7.cloned.1.call-start = ((), (), s32[]{:S(2)}) async-start(), calls=%async_computation.3 | async-start | bytes 2228224 | tf_op jit(solution)/shard_map/all_gather | solution.py:77
  229.2 195.1 %all-gather.11.cloned.1.call-start = ((), (), s32[]{:S(2)}) async-start(), calls=%async_computation.5 | async-start | bytes 6291456 | tf_op jit(solution)/shard_map/all_gather | solution.py:79
  (30 other events, 127.9 us)
Sparse Core Ops, SparseCore 0:
  19.3 89.2 all-gather.4
  175.6 39.6 reduce-scatter.1
  228.7 53.9 all-gather.8
  284.6 62.6 all-gather.6
  349.2 75.0 all-gather.10
